TPU v7x, 256 devices: a whole 4x4x8 slice. The times are simulated.
256 devices in a mesh: blk: 32 (over x_lo, z, core), tp: 8 (over y, x_hi).
Axes of the slice: x: 4 (x_hi: 2, x_lo: 2; x = x_hi * 2 + x_lo), y: 4, z: 8, core: 2. Of those that a mesh axis runs over, the one named last changes fastest.
Arguments:
- hidden_in: bfloat16 [12288, 4096], P('blk'), may hold values from -6 to 6
- w_query: bfloat16 [4096, 4096], P('blk', 'tp'), may hold values from -0.09375 to 0.09375
- w_key: bfloat16 [4096, 1024], P('blk', 'tp'), may hold values from -0.09375 to 0.09375
- w_value: bfloat16 [4096, 1024], P('blk', 'tp'), may hold values from -0.09375 to 0.09375
- starts: int32 [32], P('blk'), may hold values from 0 to 1152, as said below
- key_cache: bfloat16 [32, 1152, 1024], P('blk', None, 'tp'), may hold values from -400 to 400
- value_cache: bfloat16 [32, 1152, 1024], P('blk', None, 'tp'), may hold values from -6 to 6
- grad_out: bfloat16 [12288, 4096], P('blk', 'tp'), may hold values from -6 to 6
Outputs:
- attended: bfloat16 [12288, 4096], P('blk', 'tp')
- grad_in: bfloat16 [12288, 4096], P('blk', 'tp')
- grad_wq: float32 [4096, 4096], P('blk', 'tp')
- grad_wk: float32 [4096, 1024], P('blk', 'tp')
- grad_wv: float32 [4096, 1024], P('blk', 'tp')
Inputs may be any that keep to these rules, and one draw needn't show every extreme that they name: `starts`: every entry is a multiple of 384; both 0 and 1152 occur.
All inputs are finite; a program needn't handle non-finite values.
Results may differ from a plain program's by a relative error of at most 0.025.
The roundings to bfloat16 on the way count: a program that leaves them out, or rounds other values in their place, can miss the bound.
Values may be sent and summed in bfloat16 or wider, within the bound.
No kernel may reach another device: no remote copies, remote signals or barrier semaphores. Data moves between devices by JAX's collectives and lax.ppermute only.
A program may use at most 128 MiB of HBM per device.

v0:
```python
import jax
import jax.numpy as jnp
from jax import lax
from jax.sharding import PartitionSpec as P

H = 32
KV = 8
HD = 128


def contract_last(left, right):
    return lax.dot_general(
        left, right, (((1,), (1,)), ((), ())), preferred_element_type=jnp.float32
    )


def contract_first(left, right):
    return lax.dot_general(
        left, right, (((0,), (0,)), ((), ())), preferred_element_type=jnp.float32
    )


def head_pass(queries, cache_keys, cache_values, fresh_keys, fresh_values, grad_heads, offset):
    groups, row_count, head_width = queries.shape
    cached = cache_keys.shape[0]
    factor = head_width ** (-0.5)
    key_list = jnp.concatenate([cache_keys, fresh_keys], 0)
    value_list = jnp.concatenate([cache_values, fresh_values], 0)
    flat_query = queries.reshape(groups * row_count, head_width)
    flat_grad = grad_heads.reshape(groups * row_count, head_width)
    scores = contract_last(flat_query, key_list) * factor
    scores = scores.reshape(groups, row_count, cached + row_count)
    row_pos = lax.iota(jnp.int32, row_count)
    cache_ok = jnp.broadcast_to(lax.iota(jnp.int32, cached)[None, :] < offset, (row_count, cached))
    own_ok = row_pos[None, :] <= row_pos[:, None]
    allowed = jnp.concatenate([cache_ok, own_ok], 1)
    scores = jnp.where(allowed[None], scores, -jnp.inf)
    row_max = jnp.max(scores, axis=-1, keepdims=True)
    expo = jnp.exp(scores - row_max)
    probs = (expo / jnp.sum(expo, axis=-1, keepdims=True)).astype(jnp.bfloat16)
    probs = probs.reshape(groups * row_count, cached + row_count)
    attended = jnp.dot(probs, value_list, preferred_element_type=jnp.float32).astype(jnp.bfloat16)
    grad_probs = contract_last(flat_grad, value_list)
    probs_wide = probs.astype(jnp.float32)
    row_dot = jnp.sum(probs_wide * grad_probs, axis=-1, keepdims=True)
    grad_scores = (probs_wide * (grad_probs - row_dot) * factor).astype(jnp.bfloat16)
    grad_query = jnp.dot(grad_scores, key_list, preferred_element_type=jnp.float32).astype(
        jnp.bfloat16
    )
    grad_keys = contract_first(grad_scores[:, cached:], flat_query).astype(jnp.bfloat16)
    grad_values = contract_first(probs[:, cached:], flat_grad).astype(jnp.bfloat16)
    return (
        attended.reshape(groups, row_count, head_width),
        grad_query.reshape(groups, row_count, head_width),
        grad_keys,
        grad_values,
    )


def local(hidden_in, w_query, w_key, w_value, starts, key_cache, value_cache, grad_out):
    tokens_dev = hidden_in.shape[0]
    kv_local = w_key.shape[1] // HD
    group = H // KV
    cached = key_cache.shape[1]
    full_query, full_key, full_value = (
        lax.all_gather(w_query, "blk", axis=0, tiled=True),
        lax.all_gather(w_key, "blk", axis=0, tiled=True),
        lax.all_gather(w_value, "blk", axis=0, tiled=True),
    )
    proj_query = jnp.dot(hidden_in, full_query, preferred_element_type=jnp.float32)
    proj_key = jnp.dot(hidden_in, full_key, preferred_element_type=jnp.float32)
    proj_value = jnp.dot(hidden_in, full_value, preferred_element_type=jnp.float32)
    queries = proj_query.astype(jnp.bfloat16)
    new_keys = proj_key.astype(jnp.bfloat16)
    new_values = proj_value.astype(jnp.bfloat16)
    per_query = queries.reshape(tokens_dev, kv_local, group, HD).transpose(1, 2, 0, 3)
    per_grad = grad_out.reshape(tokens_dev, kv_local, group, HD).transpose(1, 2, 0, 3)
    cache_k = key_cache[0].reshape(cached, kv_local, HD).transpose(1, 0, 2)
    cache_v = value_cache[0].reshape(cached, kv_local, HD).transpose(1, 0, 2)
    fresh_k = new_keys.reshape(tokens_dev, kv_local, HD).transpose(1, 0, 2)
    fresh_v = new_values.reshape(tokens_dev, kv_local, HD).transpose(1, 0, 2)
    offset = starts[0]
    results = lax.map(
        lambda packed: head_pass(*packed, offset),
        (per_query, cache_k, cache_v, fresh_k, fresh_v, per_grad),
    )
    attended = results[0].transpose(2, 0, 1, 3).reshape(tokens_dev, kv_local * group * HD)
    grad_query = results[1].transpose(2, 0, 1, 3).reshape(tokens_dev, kv_local * group * HD)
    grad_keys = results[2].transpose(1, 0, 2).reshape(tokens_dev, kv_local * HD)
    grad_values = results[3].transpose(1, 0, 2).reshape(tokens_dev, kv_local * HD)
    input_term = (
        contract_last(grad_query, full_query)
        + contract_last(grad_keys, full_key)
        + contract_last(grad_values, full_value)
    )
    grad_in = lax.psum_scatter(input_term, "tp", scatter_dimension=1, tiled=True).astype(
        jnp.bfloat16
    )
    grads_cat = jnp.concatenate([grad_query, grad_keys, grad_values], 1)
    blk_count = lax.axis_size("blk")
    summed = lax.psum_scatter(
        contract_first(hidden_in, grads_cat), "blk", scatter_dimension=0, tiled=True
    )
    summed = summed * (tokens_dev * blk_count) ** (-0.5)
    query_cols = w_query.shape[1]
    kv_cols = w_key.shape[1]
    grad_wq = summed[:, :query_cols]
    grad_wk = summed[:, query_cols : query_cols + kv_cols]
    grad_wv = summed[:, query_cols + kv_cols :]
    return (attended, grad_in, grad_wq, grad_wk, grad_wv)


def solution(mesh):
    in_specs = (
        P("blk", None),
        P("blk", "tp"),
        P("blk", "tp"),
        P("blk", "tp"),
        P("blk"),
        P("blk", None, "tp"),
        P("blk", None, "tp"),
        P("blk", "tp"),
    )
    out_specs = (P("blk", "tp"), P("blk", "tp"), P("blk", "tp"), P("blk", "tp"), P("blk", "tp"))
    return jax.shard_map(local, mesh=mesh, in_specs=in_specs, out_specs=out_specs, check_vma=False)
```

profile of v0, /device:TPU:16, one launch (start us, length us, event | category | flops | bytes accessed | tf_op | source)
XLA Modules:
  0.0 504.6 jit_solution(6510871509543316294)
XLA Ops:
  10.1 1.2 copy.27
  12.6 2.2 broadcast_in_dim.55
  14.8 2.6 copy.33
  17.4 58.8 %all-gather.8.cloned.1.call-done = bf16[4096,128]{1,0:T(8,128)(2,1)} async-done(((bf16[128,128]{1,0:T(8,128)(2,1)}), bf16[4096,128]{1,0:T(8,128)(2,1)}) %all-gather.8.cloned.1.call-update) | async-done | bytes 1048592 | tf_op jit(solution)/shard_map/all_gather | solution.py:68
  76.2 2.8 convolution_convert_fusion.3
  79.0 62.3 %all-gather.6.cloned.1.call-done = bf16[4096,128]{1,0:T(8,128)(2,1)} async-done(((bf16[128,128]{1,0:T(8,128)(2,1)}), bf16[4096,128]{1,0:T(8,128)(2,1)}) %all-gather.6.cloned.1.call-update) | async-done | bytes 1048592 | tf_op jit(solution)/shard_map/all_gather | solution.py:67
  141.3 2.8 convolution_convert_fusion.4
  144.2 65.3 %all-gather.4.cloned.1.call-done = bf16[4096,512]{1,0:T(8,128)(2,1)} async-done(((bf16[128,512]{1,0:T(8,128)(2,1)}), bf16[4096,512]{1,0:T(8,128)(2,1)}) %all-gather.4.cloned.1.call-update) | async-done | bytes 4194320 | tf_op jit(solution)/shard_map/all_gather | solution.py:66
  209.5 4.7 convolution_convert_fusion.2
  215.4 3.6 fusion.27
  219.0 1.3 fusion.4
  220.3 5.0 fusion.1
  225.4 1.5 fusion.12
  226.9 8.0 %fusion.3 = bf16[1536,1536]{0,1:T(8,128)(2,1)} fusion(bf16[1536,1536]{0,1:T(8,128)(2,1)S(1)} %get-tuple-element.57, f32[1536,1536]{1,0:T(8,128)} %get-tuple-element.62, f32[1536]{0:T(1024)S(1)} %get-tuple-element.56), kind=kLoop, calls=%fused_computation.6 | loop fusion | flops 11796480 | bytes 18880512 | tf_op jit(solution)/shard_map/while/body/eval_jaxpr/convert_element_type | solution.py:46
  234.9 2.4 fusion.9
  237.3 4.5 convolution_convert_fusion
  241.8 1.2 copy.29
  243.1 4.1 fusion.28
  248.5 3.7 add_add_fusion
  252.3 7.3 %convolution_bitcast_fusion = f32[4096,768]{0,1:T(8,128)} fusion(bf16[384,4096]{1,0:T(8,128)(2,1)S(1)} %copy-done, bf16[384,128]{0,1:T(8,128)(2,1)} %fusion.12, bf16[384,128]{0,1:T(8,128)(2,1)} %fusion.9, bf16[384,512]{0,1:T(8,128)(2,1)S(1)} %bitcast.56), kind=kOutput, calls=%fused_computation.11 | convolution fusion | flops 2417688576 | bytes 16318464 | tf_op jit(solution)/shard_map/dot_general | solution.py:18
  260.6 3.8 convolution_convert_fusion.1
  265.5 88.7 %reduce-scatter.3.cloned.1.call-done = f32[384,512]{1,0:T(8,128)} async-done(((f32[384,4096]{1,0:T(8,128)}), f32[384,512]{1,0:T(8,128)}) %reduce-scatter.3.cloned.1.call-update) | async-done | bytes 786448 | tf_op jit(solution)/shard_map/reduce_scatter | solution.py:96
  354.2 1.9 convert_element_type.51
  356.1 138.6 %reduce-scatter.5.cloned.1.call-done = f32[128,768]{0,1:T(8,128)} async-done(((f32[4096,768]{0,1:T(8,128)}), f32[128,768]{0,1:T(8,128)}) %reduce-scatter.5.cloned.1.call-update) | async-done | bytes 393232 | tf_op jit(solution)/shard_map/reduce_scatter | solution.py:101
  (52 shorter events, 11.4 us)
Async XLA Ops:
  7.2 69.0 %copy-start = (bf16[384,4096]{1,0:T(8,128)(2,1)S(1)}, bf16[384,4096]{1,0:T(8,128)(2,1)}, u32[]{:S(2)}) copy-start(bf16[384,4096]{1,0:T(8,128)(2,1)} %param.8) | copy-start | bytes 9437188
  7.2 69.0 %all-gather.8.cloned.1.call-start = ((), (), s32[]{:S(2)}) async-start(), calls=%async_computation.4 | async-start | bytes 1081344 | tf_op jit(solution)/shard_map/all_gather | solution.py:68
  7.9 133.4 %all-gather.6.cloned.1.call-start = ((), (), s32[]{:S(2)}) async-start(), calls=%async_computation.3 | async-start | bytes 1081344 | tf_op jit(solution)/shard_map/all_gather | solution.py:67
  8.7 200.8 %all-gather.4.cloned.1.call-start = ((), (), s32[]{:S(2)}) async-start(), calls=%async_computation.2 | async-start | bytes 4325376 | tf_op jit(solution)/shard_map/all_gather | solution.py:66
  9.4 344.8 %reduce-scatter.3.cloned.1.call-start = ((), (), s32[]{:S(2)}) async-start(), calls=%async_computation.5 | async-start | bytes 7077888 | tf_op jit(solution)/shard_map/reduce_scatter | solution.py:96
  218.9 1.4 copy-start.6
  218.9 1.4 copy-start.7
  218.9 1.4 copy-start.11
  225.4 9.6 %copy-start.1 = (bf16[1536,1536]{0,1:T(8,128)(2,1)}, bf16[1536,1536]{0,1:T(8,128)(2,1)S(1)}, u32[]{:S(2)}) copy-start(bf16[1536,1536]{0,1:T(8,128)(2,1)S(1)} %get-tuple-element.57) | copy-start | bytes 14155780
  226.9 10.4 %copy-start.9 = (bf16[384,128]{1,0:T(8,128)(2,1)S(1)}, bf16[384,128]{1,0:T(8,128)(2,1)}, u32[]{:S(2)}) copy-start(bf16[384,128]{1,0:T(8,128)(2,1)} %convolution_convert_fusion.4) | copy-start | bytes 294916
  226.9 10.4 %copy-start.10 = (bf16[1,1152,128]{2,1,0:T(8,128)(2,1)S(1)}, bf16[1,1152,128]{2,1,0:T(8,128)(2,1)}, u32[]{:S(2)}) copy-start(bf16[1,1152,128]{2,1,0:T(8,128)(2,1)} %param.13) | copy-start | bytes 884740
  243.1 4.2 copy-start.3
  243.1 4.2 copy-start.4
  247.2 1.2 copy-start.2
  247.2 1.2 copy-start.5
  252.2 242.5 %reduce-scatter.5.cloned.1.call-start = ((), (), s32[]{:S(2)}) async-start(), calls=%async_computation.6 | async-start | bytes 12976128 | tf_op jit(solution)/shard_map/reduce_scatter | solution.py:101
  259.6 0.9 copy-start.8
  259.6 1.0 copy-start.12
Sparse Core Ops, SparseCore 0:
  9.8 66.3 all-gather.7
  78.0 63.2 all-gather.5
  143.2 66.2 all-gather.3
  252.3 101.7 reduce-scatter.2
  356.6 138.0 reduce-scatter.4
where the time goes:
time: 505 us
  waiting for transfers between devices  416 us (82%)
  matrix products  47.4 us (9%)
  between operations  14.6 us (3%)
  local copies, waits for them, and re-layouts  14 us (3%)
  other arithmetic  12.6 us (2%)
    reduce_scatter x1, waiting for transfers between devices, local(): lax.psum_scatter(contract_first(hidden_in, grads_cat), 'blk', scatter_dim...  139 us
    reduce_scatter x1, waiting for transfers between devices, local(): lax.psum_scatter(input_term, 'tp', scatter_dimension=1, tiled=True)  88.7 us
    all_gather x1, waiting for transfers between devices, local(): lax.all_gather(w_query, 'blk', axis=0, tiled=True)  65.3 us
    all_gather x1, waiting for transfers between devices, local(): lax.all_gather(w_key, 'blk', axis=0, tiled=True)  62.3 us
    all_gather x1, waiting for transfers between devices, local(): lax.all_gather(w_value, 'blk', axis=0, tiled=True)  58.8 us
    dot_general x5, matrix products, contract_last(): lax.dot_general(left, right, (((1,), (1,)), ((), ())), preferred_element_...  17.5 us
    dot_general x3, matrix products, contract_first(): lax.dot_general(left, right, (((0,), (0,)), ((), ())), preferred_element_...  11.3 us
  transfers between devices with their start and end apart: 5, of which 5 were waited for; matrix products, arithmetic and copies ran while one was open for 5% of the time, Pallas kernels for 0%

commit v1 on v0

--- a/solution.py
+++ b/solution.py
@@ -63,7 +63,9 @@
     group = H // KV
     cached = key_cache.shape[1]
     full_query, full_key, full_value = (
-        lax.all_gather(w_query, "blk", axis=0, tiled=True),
+        jnp.concatenate(
+            lax.all_to_all(jnp.stack([w_query] * lax.axis_size("blk")), "blk", 0, 0), axis=0
+        ),
         lax.all_gather(w_key, "blk", axis=0, tiled=True),
         lax.all_gather(w_value, "blk", axis=0, tiled=True),
     )

time: 505 us -> 463 us (0.917)
  waiting for transfers between devices: 416 us -> 360 us
  starting transfers between devices: 0.19 us -> 10.1 us
    all_gather x1 -> x0, waiting for transfers between devices: 65.3 us -> none  [local(): lax.all_gather(w_query, 'blk', axis=0, tiled=True)]
    all_to_all x0 -> x1, starting transfers between devices: none -> 9.91 us  [local(): lax.all_to_all(jnp.stack([w_query] * lax.axis_size('blk')), 'blk', 0, 0)]
    all_gather x1, waiting for transfers between devices: 58.8 us -> 66.7 us  [local(): lax.all_gather(w_value, 'blk', axis=0, tiled=True)]
  transfers between devices with their start and end apart: 5 -> 5, of which waited for: 5 -> 4; matrix products, arithmetic and copies ran while one was open for 5% -> 6% of each run, Pallas kernels for 0% -> 0%
where the time goes in v1:
time: 463 us; the launch traced here: 462 us
  waiting for transfers between devices  360 us (78%)
  matrix products  47.4 us (10%)
  local copies, waits for them, and re-layouts  17.5 us (4%)
  between operations  14.6 us (3%)
  other arithmetic  12.6 us (3%)
  starting transfers between devices  10.1 us (2%)
    reduce_scatter x1, waiting for transfers between devices, local(): lax.psum_scatter(contract_first(hidden_in, grads_cat), 'blk', scatter_dim...  138 us
    reduce_scatter x1, waiting for transfers between devices, local(): lax.psum_scatter(input_term, 'tp', scatter_dimension=1, tiled=True)  88.3 us
    all_gather x1, waiting for transfers between devices, local(): lax.all_gather(w_value, 'blk', axis=0, tiled=True)  66.7 us
    all_gather x1, waiting for transfers between devices, local(): lax.all_gather(w_key, 'blk', axis=0, tiled=True)  65.7 us
    dot_general x5, matrix products, contract_last(): lax.dot_general(left, right, (((1,), (1,)), ((), ())), preferred_element_...  17.5 us
    dot_general x3, matrix products, contract_first(): lax.dot_general(left, right, (((0,), (0,)), ((), ())), preferred_element_...  11.2 us
    all_to_all x1, starting transfers between devices, local(): lax.all_to_all(jnp.stack([w_query] * lax.axis_size('blk')), 'blk', 0, 0)  9.91 us
  transfers between devices with their start and end apart: 5, of which 4 were waited for; matrix products, arithmetic and copies ran while one was open for 6% of the time, Pallas kernels for 0%

profile of v1, /device:TPU:16, one launch (start us, length us, event | category | flops | bytes accessed | tf_op | source)
XLA Modules:
  0.0 462.5 jit_solution(9318687529128566444)
XLA Ops:
  7.2 3.5 stack.2
  10.7 9.9 %all-to-all-start = ((bf16[32,128,512]{2,1,0:T(8,128)(2,1)}), bf16[32,128,512]{2,1,0:T(8,128)(2,1)}, u32[]{:S(2)}, u32[]{:S(2)}) async-start(bf16[32,128,512]{2,1,0:T(8,128)(2,1)} %stack.2), calls=%async_computation | async-start | bytes 8388608 | tf_op jit(solution)/shard_map/all_to_all | solution.py:67
  22.7 1.2 copy.27
  25.3 2.2 broadcast_in_dim.55
  27.5 2.7 copy.33
  30.1 66.7 %all-gather.5.cloned.1.call-done = bf16[4096,128]{1,0:T(8,128)(2,1)} async-done(((bf16[128,128]{1,0:T(8,128)(2,1)}), bf16[4096,128]{1,0:T(8,128)(2,1)}) %all-gather.5.cloned.1.call-update) | async-done | bytes 1048592 | tf_op jit(solution)/shard_map/all_gather | solution.py:70
  96.8 2.8 convolution_convert_fusion.3
  99.7 65.7 %all-gather.3.cloned.1.call-done = bf16[4096,128]{1,0:T(8,128)(2,1)} async-done(((bf16[128,128]{1,0:T(8,128)(2,1)}), bf16[4096,128]{1,0:T(8,128)(2,1)}) %all-gather.3.cloned.1.call-update) | async-done | bytes 1048592 | tf_op jit(solution)/shard_map/all_gather | solution.py:69
  165.4 2.8 convolution_convert_fusion.4
  168.2 4.7 %convolution_convert_fusion.2 = bf16[384,512]{1,0:T(8,128)(2,1)} fusion(bf16[384,4096]{1,0:T(8,128)(2,1)S(1)} %copy-done, bf16[4096,512]{1,0:T(8,128)(2,1)} %bitcast.1), kind=kOutput, calls=%fused_computation.16 | convolution fusion | flops 1610809344 | bytes 7733248 | tf_op jit(solution)/shard_map/dot_general | solution.py:72
  174.1 3.6 fusion.27
  177.7 1.3 fusion.4
  179.0 5.0 %fusion.1 = (f32[1536]{0:T(1024)S(1)}, bf16[1536,1536]{0,1:T(8,128)(2,1)S(1)}, f32[1536,1536]{1,0:T(8,128)}) fusion(f32[1536]{0:T(1024)S(1)} %fusion.4, f32[1536,1536]{0,1:T(8,128)S(1)} %get-tuple-element.61, f32[1536]{0:T(1024)S(1)} %get-tuple-element.60, bf16[1536,128]{1,0:T(8,128)(2,1)S(1)} %bitcast.61, bf16[384,128]{1,0:T(8,128)(2,1)S(1)} %copy-done.7, ...), kind=kOutput, calls=%fused_computation.4 | convolution fusion | flops 618920448 | bytes 24397824 | tf_op jit(solution)/shard_map/while/body/eval_jaxpr/dot_general | solution.py:12
  184.1 1.5 fusion.12
  185.6 8.0 %fusion.3 = bf16[1536,1536]{0,1:T(8,128)(2,1)} fusion(bf16[1536,1536]{0,1:T(8,128)(2,1)S(1)} %get-tuple-element.57, f32[1536,1536]{1,0:T(8,128)} %get-tuple-element.62, f32[1536]{0:T(1024)S(1)} %get-tuple-element.56), kind=kLoop, calls=%fused_computation.6 | loop fusion | flops 11796480 | bytes 18880512 | tf_op jit(solution)/shard_map/while/body/eval_jaxpr/convert_element_type | solution.py:46
  193.6 2.4 fusion.9
  196.1 4.5 convolution_convert_fusion
  201.8 4.1 fusion.28
  207.2 3.7 add_add_fusion
  211.0 7.3 %convolution_bitcast_fusion = f32[4096,768]{0,1:T(8,128)} fusion(bf16[384,4096]{1,0:T(8,128)(2,1)S(1)} %copy-done, bf16[384,128]{0,1:T(8,128)(2,1)} %fusion.12, bf16[384,128]{0,1:T(8,128)(2,1)} %fusion.9, bf16[384,512]{0,1:T(8,128)(2,1)S(1)} %bitcast.57), kind=kOutput, calls=%fused_computation.11 | convolution fusion | flops 2417688576 | bytes 16318464 | tf_op jit(solution)/shard_map/dot_general | solution.py:18
  219.3 3.8 convolution_convert_fusion.1
  224.1 88.3 %reduce-scatter.3.cloned.1.call-done = f32[384,512]{1,0:T(8,128)} async-done(((f32[384,4096]{1,0:T(8,128)}), f32[384,512]{1,0:T(8,128)}) %reduce-scatter.3.cloned.1.call-update) | async-done | bytes 786448 | tf_op jit(solution)/shard_map/reduce_scatter | solution.py:98
  312.5 1.9 convert_element_type.51
  314.4 138.2 %reduce-scatter.5.cloned.1.call-done = f32[128,768]{0,1:T(8,128)} async-done(((f32[4096,768]{0,1:T(8,128)}), f32[128,768]{0,1:T(8,128)}) %reduce-scatter.5.cloned.1.call-update) | async-done | bytes 393232 | tf_op jit(solution)/shard_map/reduce_scatter | solution.py:103
  (52 shorter events, 11.9 us)
Async XLA Ops:
  7.2 89.7 %copy-start = (bf16[384,4096]{1,0:T(8,128)(2,1)S(1)}, bf16[384,4096]{1,0:T(8,128)(2,1)}, u32[]{:S(2)}) copy-start(bf16[384,4096]{1,0:T(8,128)(2,1)} %param.8) | copy-start | bytes 9437188
  10.7 157.6 %all-to-all-start = ((bf16[32,128,512]{2,1,0:T(8,128)(2,1)}), bf16[32,128,512]{2,1,0:T(8,128)(2,1)}, u32[]{:S(2)}, u32[]{:S(2)}) async-start(bf16[32,128,512]{2,1,0:T(8,128)(2,1)} %stack.2), calls=%async_computation | async-start | bytes 8388608 | tf_op jit(solution)/shard_map/all_to_all | solution.py:67
  20.6 76.3 %all-gather.5.cloned.1.call-start = ((), (), s32[]{:S(2)}) async-start(), calls=%async_computation.4 | async-start | bytes 1081344 | tf_op jit(solution)/shard_map/all_gather | solution.py:70
  21.3 144.1 %all-gather.3.cloned.1.call-start = ((), (), s32[]{:S(2)}) async-start(), calls=%async_computation.3 | async-start | bytes 1081344 | tf_op jit(solution)/shard_map/all_gather | solution.py:69
  22.1 290.4 %reduce-scatter.3.cloned.1.call-start = ((), (), s32[]{:S(2)}) async-start(), calls=%async_computation.5 | async-start | bytes 7077888 | tf_op jit(solution)/shard_map/reduce_scatter | solution.py:98
  177.7 1.4 copy-start.6
  177.7 1.4 copy-start.7
  177.7 1.4 copy-start.11
  184.1 9.5 %copy-start.1 = (bf16[1536,1536]{0,1:T(8,128)(2,1)}, bf16[1536,1536]{0,1:T(8,128)(2,1)S(1)}, u32[]{:S(2)}) copy-start(bf16[1536,1536]{0,1:T(8,128)(2,1)S(1)} %get-tuple-element.57) | copy-start | bytes 14155780
  185.6 10.4 %copy-start.9 = (bf16[384,128]{1,0:T(8,128)(2,1)S(1)}, bf16[384,128]{1,0:T(8,128)(2,1)}, u32[]{:S(2)}) copy-start(bf16[384,128]{1,0:T(8,128)(2,1)} %convolution_convert_fusion.4) | copy-start | bytes 294916
  185.6 10.4 %copy-start.10 = (bf16[1,1152,128]{2,1,0:T(8,128)(2,1)S(1)}, bf16[1,1152,128]{2,1,0:T(8,128)(2,1)}, u32[]{:S(2)}) copy-start(bf16[1,1152,128]{2,1,0:T(8,128)(2,1)} %param.13) | copy-start | bytes 884740
  201.8 4.2 copy-start.3
  201.8 4.2 copy-start.4
  206.0 1.2 copy-start.2
  206.0 1.2 copy-start.5
  210.9 241.7 %reduce-scatter.5.cloned.1.call-start = ((), (), s32[]{:S(2)}) async-start(), calls=%async_computation.6 | async-start | bytes 12976128 | tf_op jit(solution)/shard_map/reduce_scatter | solution.py:103
  218.2 0.9 copy-start.8
  218.2 1.0 copy-start.12
Sparse Core Ops, SparseCore 0:
  23.2 73.5 all-gather.4
  98.7 66.6 all-gather.2
  211.0 101.3 reduce-scatter.2
  314.9 137.6 reduce-scatter.4
